TPU v7x, 32 devices: a whole 2x2x4 slice. The times are simulated.
32 devices in a mesh: dp: 4 (over y, x), expert: 8 (over z, core).
Axes of the slice: x: 2, y: 2, z: 4, core: 2. Of those that a mesh axis runs over, the one named last changes fastest.
Arguments:
- hidden: bfloat16 [32, 2048], P(('dp', 'expert')), may hold values from -6 to 6
- attn_gain: float32 [2048], replicated, may hold values from 0.25 to 1.75
- query_weight: bfloat16 [3072, 2048], P('expert'), may hold values from -0.125 to 0.125
- latent_down: bfloat16 [2048, 576], replicated, may hold values from -0.125 to 0.125
- latent_up: bfloat16 [512, 4096], P(None, 'expert'), may hold values from -0.25 to 0.25
- out_weight: bfloat16 [2048, 2048], P('expert'), may hold values from -0.125 to 0.125
- latent_pool: bfloat16 [128, 32, 576], P('dp'), may hold values from -1000 to 1000
- page_table: int32 [32, 16], replicated, may hold values from -1 to 127, as said below
- page_counts: int32 [32], replicated, may hold values from 1 to 16, as said below
- ffn_gain: float32 [2048], replicated, may hold values from 0.25 to 1.75
- expert_ids: int32 [32, 6], replicated, may hold values from 0 to 23, all different within a row; in each aligned block of 32 rows (0 to 31, 32 to 63, ...) at most 16 rows name the same one
- expert_gates: float32 [32, 6], replicated, may hold values from 0.05 to 0.6
- old_place: int32 [8, 4], replicated, may hold values from 0 to 23, as said below
- new_place: int32 [8, 4], replicated, may hold values from 0 to 23, as said below
- expert_gate_up: bfloat16 [32, 2, 1408, 2048], P('expert', None, None, 'dp'), as said below
- expert_down: bfloat16 [32, 1408, 2048], P('expert', None, 'dp'), as said below
- shared_gate_up: bfloat16 [2, 2816, 2048], P(None, None, 'dp'), may hold values from -0.125 to 0.125
- shared_down: bfloat16 [2816, 2048], P(None, 'dp'), may hold values from -0.109375 to 0.109375
Outputs:
- layer_out: bfloat16 [32, 2048], P(('dp', 'expert'))
- moved_gate_up: bfloat16 [32, 2, 1408, 2048], P('expert', None, None, 'dp')
- moved_down: bfloat16 [32, 1408, 2048], P('expert', None, 'dp')
Inputs may be any that keep to these rules, and one draw needn't show every extreme that they name: `page_counts`: each request's count of cached pages; exactly one request has 16. `page_table`: row t names page_counts[t] pages of the pool, no page named twice in the table; its other entries are -1. Page p lies on dp index p // 32. `expert_ids`: no expert is named by more than 16 tokens in all; some expert by exactly 16. `old_place`: row i holds the experts of the slots on expert index i, slot s of row i being global slot i * 4 + s; every expert is held by one slot or more. `new_place`: equal to old_place except in exactly one slot of each row, which names another expert. `expert_gate_up`: slots that hold the same expert under old_place hold equal weights. `expert_down`: slots that hold the same expert under old_place hold equal weights.
All inputs are finite; a program needn't handle non-finite values.
Results may differ from a plain program's by a relative error of at most 0.02.
Values may be sent and summed in bfloat16 or wider, within the bound.
No kernel may reach another device: no remote copies, remote signals or barrier semaphores. Data moves between devices by JAX's collectives and lax.ppermute only.
A program may use at most 128 MiB of HBM per device.

v0:
```python
import math
import jax
import jax.numpy as jnp
from jax import lax
from jax.sharding import PartitionSpec as P

NOPE = 128
ROPE = 64
VHEAD = 128
LATENT = 512
EXP_DEV = 3
PAGE = 32
EPSILON = 1e-06
ROPE_BASE = 50000.0
MASKED_SCORE = -1e30
HIGHEST = lax.Precision.HIGHEST


def rms_plain(values):
    mean_square = jnp.mean(values * values, axis=-1, keepdims=True)
    return values * lax.rsqrt(mean_square + EPSILON)


def rms_norm(values, norm_gain):
    return rms_plain(values) * norm_gain


def rotary(values, position):
    half_width = values.shape[-1] // 2
    exponent = jnp.arange(half_width).astype(jnp.float32) * (2.0 / values.shape[-1])
    frequency = jnp.exp(-exponent * math.log(ROPE_BASE))
    angles = position[..., None] * frequency
    cosine = jnp.cos(angles)
    sine_part = jnp.sin(angles)
    first_half = values[..., :half_width]
    second = values[..., half_width:]
    return jnp.concatenate(
        [first_half * cosine - second * sine_part, second * cosine + first_half * sine_part],
        axis=-1,
    )


def gather_rows(rows):
    by_expert = lax.all_gather(rows, "expert", axis=0, tiled=True)
    return lax.all_gather(by_expert, "dp", axis=0, tiled=True)


def spread_slots(gate_up, down, picks, ex_count):
    chosen = jnp.concatenate([gate_up[picks], down[picks][:, None]], axis=1)
    count, parts, ff_width, col_width = chosen.shape
    pieces = chosen.reshape(count, parts, ex_count, ff_width // ex_count, col_width)
    spread = lax.all_to_all(pieces, "expert", split_axis=2, concat_axis=0, tiled=True)
    return spread.reshape(ex_count * count, parts, ff_width // ex_count, col_width)


def migrate(expert_gate_up, expert_down, old_place, new_place, ex_index):
    rows, slots_local = old_place.shape
    slots = rows * slots_local
    ex_count = rows
    ff_width = expert_gate_up.shape[2]
    changed = old_place != new_place
    moved_slot = jnp.argmax(changed, axis=1)
    wanted = jnp.take_along_axis(new_place, moved_slot[:, None], axis=1)[:, 0]
    hit = old_place.reshape(-1)[None, :] == wanted[:, None]
    first = jnp.argmax(hit, axis=1).astype(jnp.int32)
    last = (slots - 1 - jnp.argmax(hit[:, ::-1], axis=1)).astype(jnp.int32)
    slot_ids = jnp.arange(slots, dtype=jnp.int32)

    def needed_of(src):
        needed = jnp.any(src[:, None] == slot_ids[None, :], axis=0).reshape(rows, slots_local)
        return (needed, jnp.max(jnp.sum(needed.astype(jnp.int32), axis=1)))

    need_first, load_first = needed_of(first)
    need_last, load_last = needed_of(last)
    use_last = load_last < load_first
    source = jnp.where(use_last, last, first)
    needed = jnp.where(use_last, need_last, need_first)
    load = jnp.minimum(load_first, load_last)
    rank = jnp.cumsum(needed.astype(jnp.int32), axis=1) - 1
    local_ids = jnp.arange(slots_local, dtype=jnp.int32)
    picks = jnp.stack(
        [jnp.argmax(needed & (rank == k), axis=1).astype(jnp.int32) for k in range(slots_local)],
        axis=1,
    )
    my_picks = picks[ex_index]
    src_dev = source // slots_local
    src_rank = rank.reshape(-1)[source]
    fast = min(2, slots_local)
    spread_a = spread_slots(expert_gate_up, expert_down, my_picks[:fast], ex_count)
    out_a = spread_a[src_dev * fast + jnp.minimum(src_rank, fast - 1)]
    if slots_local > fast:
        rest = slots_local - fast

        def extra():
            spread_b = spread_slots(expert_gate_up, expert_down, my_picks[fast:], ex_count)
            return spread_b[src_dev * rest + jnp.clip(src_rank - fast, 0, rest - 1)]

        out_b = lax.cond(load > fast, extra, lambda: jnp.zeros_like(out_a))
        out_a = jnp.where((src_rank < fast)[:, None, None, None], out_a, out_b)
    arrived = lax.all_to_all(out_a, "expert", split_axis=0, concat_axis=2, tiled=True)
    is_moved = local_ids == moved_slot[ex_index]
    moved_gate_up = jnp.where(is_moved[:, None, None, None], arrived[:, :2], expert_gate_up)
    moved_down = jnp.where(is_moved[:, None, None], arrived[:, 2], expert_down)
    return (moved_gate_up, moved_down)


def local(
    hidden,
    attn_gain,
    query_weight,
    latent_down,
    latent_up,
    out_weight,
    latent_pool,
    page_table,
    page_counts,
    ffn_gain,
    expert_ids,
    expert_gates,
    old_place,
    new_place,
    expert_gate_up,
    expert_down,
    shared_gate_up,
    shared_down,
):
    dp_count = lax.axis_size("dp")
    ex_count = lax.axis_size("expert")
    dp_index = lax.axis_index("dp")
    ex_index = lax.axis_index("expert")
    req_local = hidden.shape[0]
    group_rows = req_local * ex_count
    requests = page_counts.shape[0]
    head_local = query_weight.shape[0] // (NOPE + ROPE)
    score_scale = (NOPE + ROPE) ** (-0.5)
    group_start = dp_index * group_rows
    everyone = gather_rows(hidden)
    normed = rms_norm(everyone.astype(jnp.float32), attn_gain).astype(jnp.bfloat16)
    queries = jnp.einsum(
        "td,qd->tq", normed, query_weight, preferred_element_type=jnp.float32
    ).reshape(requests, head_local, NOPE + ROPE)
    position = (page_counts * PAGE).astype(jnp.float32)
    query_rope = rotary(queries[..., NOPE:], position[:, None]).astype(jnp.bfloat16)
    up_table = latent_up.reshape(LATENT, head_local, NOPE + VHEAD)
    query_latent = jnp.einsum(
        "thn,lhn->thl",
        queries[..., :NOPE],
        up_table[..., :NOPE].astype(jnp.float32),
        precision=HIGHEST,
    ).astype(jnp.bfloat16)
    pages_local = latent_pool.shape[0]
    pool_total = pages_local * dp_count
    flat_pages = page_table.reshape(-1)
    flat_owner = jnp.repeat(jnp.arange(requests, dtype=jnp.int32), page_table.shape[1])
    target = jnp.where(flat_pages >= 0, flat_pages, pool_total)
    owner_all = jnp.full((pool_total,), -1, jnp.int32).at[target].set(flat_owner, mode="drop")
    page_owner = lax.dynamic_slice_in_dim(owner_all, dp_index * pages_local, pages_local)
    page_used = page_owner >= 0
    owner_safe = jnp.maximum(page_owner, 0)
    page_latent = latent_pool[..., :LATENT]
    page_rope = latent_pool[..., LATENT:]
    scores = jnp.einsum(
        "phl,pkl->phk", query_latent[owner_safe], page_latent, preferred_element_type=jnp.float32
    )
    scores = (
        scores
        + jnp.einsum(
            "phr,pkr->phk", query_rope[owner_safe], page_rope, preferred_element_type=jnp.float32
        )
    ) * score_scale
    raw_max = jnp.max(scores, axis=2)
    weights = jnp.exp(scores - raw_max[..., None])
    page_total = jnp.sum(weights, axis=2)
    page_mix = jnp.einsum(
        "phk,pkl->phl",
        weights.astype(jnp.bfloat16),
        page_latent,
        preferred_element_type=jnp.float32,
    )
    page_max = jnp.where(page_used[:, None], raw_max, MASKED_SCORE)
    member = page_owner[None, :] == jnp.arange(requests, dtype=jnp.int32)[:, None]
    req_max = jnp.max(jnp.where(member[:, :, None], page_max[None], MASKED_SCORE), axis=1)
    rescale = jnp.where(page_used[:, None], jnp.exp(page_max - req_max[owner_safe]), 0.0)
    member_float = member.astype(jnp.float32)
    req_total = jnp.dot(member_float, page_total * rescale, precision=HIGHEST)
    req_mix = jnp.einsum(
        "rp,phl->rhl", member_float, page_mix * rescale[..., None], precision=HIGHEST
    )
    packed = jnp.concatenate([req_mix, req_max[..., None], req_total[..., None]], axis=-1)
    gathered = lax.all_gather(packed, "dp", axis=0, tiled=False)
    gathered = lax.dynamic_slice_in_dim(gathered, group_start, group_rows, 1)
    each_max = gathered[..., LATENT]
    part_max = jnp.max(each_max, axis=0)
    each_weight = jnp.exp(each_max - part_max[None])
    part_total = jnp.sum(gathered[..., LATENT + 1] * each_weight, axis=0)
    part_mix = jnp.sum(gathered[..., :LATENT] * each_weight[..., None], axis=0)
    own_normed = lax.dynamic_slice_in_dim(normed, group_start, group_rows, 0)
    own_position = lax.dynamic_slice_in_dim(position, group_start, group_rows, 0)
    fresh_latent = jnp.dot(own_normed, latent_down, preferred_element_type=jnp.float32)
    new_latent = rms_plain(fresh_latent[:, :LATENT]).astype(jnp.bfloat16)
    new_rope = rotary(fresh_latent[:, LATENT:], own_position).astype(jnp.bfloat16)
    own_query = lax.dynamic_slice_in_dim(query_latent, group_start, group_rows, 0)
    own_rope_query = lax.dynamic_slice_in_dim(query_rope, group_start, group_rows, 0)
    own_score = jnp.einsum("thl,tl->th", own_query, new_latent, preferred_element_type=jnp.float32)
    own_score = (
        own_score
        + jnp.einsum("thr,tr->th", own_rope_query, new_rope, preferred_element_type=jnp.float32)
    ) * score_scale
    highest = jnp.maximum(part_max, own_score)
    kept_part = jnp.exp(part_max - highest)
    own_weight = jnp.exp(own_score - highest)
    denominator = part_total * kept_part + own_weight
    numerator = (
        part_mix * kept_part[..., None]
        + own_weight[..., None] * new_latent.astype(jnp.float32)[:, None, :]
    )
    attended = (numerator / denominator[..., None]).astype(jnp.bfloat16)
    heads_out = jnp.einsum(
        "thl,lhv->thv", attended, up_table[..., NOPE:], preferred_element_type=jnp.float32
    )
    heads_out = heads_out.astype(jnp.bfloat16).reshape(group_rows, head_local * VHEAD)
    partial_value = jnp.dot(heads_out, out_weight, preferred_element_type=jnp.float32)
    attn_out = lax.psum_scatter(partial_value, "expert", scatter_dimension=0, tiled=True)
    residual = hidden.astype(jnp.float32) + attn_out
    normed_ffn = rms_norm(residual, ffn_gain).astype(jnp.bfloat16)
    slots_local = expert_gate_up.shape[0]
    ff_width = expert_gate_up.shape[2]
    col_width = expert_gate_up.shape[3]
    every_row = gather_rows(normed_ffn)
    my_columns = lax.dynamic_slice_in_dim(every_row, dp_index * col_width, col_width, 1)
    by_group = my_columns.reshape(dp_count, ex_count, req_local, col_width).transpose(1, 0, 2, 3)
    ffn_rows = by_group.reshape(requests, col_width)
    column_rows = lax.dynamic_index_in_dim(by_group, ex_index, 0, keepdims=False).reshape(
        dp_count * req_local, col_width
    )
    top_count = expert_ids.shape[1]
    experts_count = EXP_DEV * ex_count
    ids_order = (
        expert_ids.reshape(dp_count, ex_count, req_local, top_count)
        .transpose(1, 0, 2, 3)
        .reshape(requests, top_count)
    )
    gates_order = (
        expert_gates.reshape(dp_count, ex_count, req_local, top_count)
        .transpose(1, 0, 2, 3)
        .reshape(requests, top_count)
    )
    old_flat = old_place.reshape(-1)
    holds_map = old_flat[None, :] == jnp.arange(experts_count, dtype=jnp.int32)[:, None]
    holder = jnp.argmax(holds_map, axis=1)
    slot_of = holder[ids_order.reshape(-1)]
    capacity = 2 * requests * top_count // experts_count
    local_slot = slot_of - ex_index * slots_local
    slot_hot = local_slot[:, None] == jnp.arange(slots_local, dtype=jnp.int32)[None, :]
    slot_rank = jnp.cumsum(slot_hot.astype(jnp.int32), axis=0) - 1
    position_in = jnp.where(slot_hot, slot_rank, capacity)
    route_hot = (
        position_in[:, :, None] == jnp.arange(capacity, dtype=jnp.int32)[None, None, :]
    ).astype(jnp.float32)
    route_hot = route_hot.reshape(requests, top_count, slots_local, capacity)
    dispatch = jnp.sum(route_hot, axis=1).astype(jnp.bfloat16)
    combine = jnp.sum(route_hot * gates_order[:, :, None, None], axis=1)
    slot_inputs = jnp.einsum(
        "tsc,td->scd", dispatch, ffn_rows, preferred_element_type=jnp.float32
    ).astype(jnp.bfloat16)
    routed_part = jnp.einsum(
        "scd,sgfd->sgcf", slot_inputs, expert_gate_up, preferred_element_type=jnp.float32
    )
    shared_part = jnp.einsum(
        "td,gfd->gtf", column_rows, shared_gate_up, preferred_element_type=jnp.float32
    )
    routed_sum, shared_sum = lax.psum((routed_part, shared_part), "dp")
    activated = (jax.nn.silu(routed_sum[:, 0]) * routed_sum[:, 1]).astype(jnp.bfloat16)
    slot_out = jnp.einsum(
        "scf,sfd->scd", activated, expert_down, preferred_element_type=jnp.float32
    )
    routed = jnp.einsum("tsc,scd->td", combine, slot_out, precision=HIGHEST)
    shared_act = (jax.nn.silu(shared_sum[0]) * shared_sum[1]).astype(jnp.bfloat16)
    shared_term = jnp.dot(shared_act, shared_down, preferred_element_type=jnp.float32)
    moe_rows = lax.psum_scatter(routed, "expert", scatter_dimension=0, tiled=True)
    moe_part = lax.all_to_all(moe_rows + shared_term, "dp", split_axis=0, concat_axis=1, tiled=True)
    layer_out = (residual + moe_part).astype(jnp.bfloat16)
    moved_gate_up, moved_down = migrate(expert_gate_up, expert_down, old_place, new_place, ex_index)
    return (layer_out, moved_gate_up, moved_down)


def solution(mesh):
    in_specs = (
        P(("dp", "expert"), None),
        P(),
        P("expert", None),
        P(),
        P(None, "expert"),
        P("expert", None),
        P("dp", None, None),
        P(),
        P(),
        P(),
        P(),
        P(),
        P(),
        P(),
        P("expert", None, None, "dp"),
        P("expert", None, "dp"),
        P(None, None, "dp"),
        P(None, "dp"),
    )
    out_specs = (P(("dp", "expert"), None), P("expert", None, None, "dp"), P("expert", None, "dp"))
    return jax.shard_map(local, mesh=mesh, in_specs=in_specs, out_specs=out_specs, check_vma=False)
```

profile of v0, /device:TPU:0, one launch (start us, length us, event | category | flops | bytes accessed | tf_op | source)
XLA Modules:
  0.0 691.7 jit_solution(8807751896408755276)
XLA Ops:
  18.1 5.9 mini-gather-slice.2
  24.0 5.2 mini-gather-slice.3
  30.6 5.2 gather_fusion.11
  35.8 4.7 gather_fusion.12
  40.5 5.0 gather_fusion.8
  45.5 5.6 pad_maximum_fusion.3
  51.1 7.7 %pad_maximum_fusion.2 = bf16[2,3,8,176,512]{4,3,2,1,0:T(8,128)(2,1)} fusion(bf16[2,1,8,176,512]{4,3,2,1,0:T(8,128)(2,1)} %bitcast.229, bf16[2,2,8,176,512]{4,3,2,1,0:T(8,128)(2,1)} %bitcast.225), kind=kLoop, calls=%fused_computation.22 | loop fusion | flops 4325376 | bytes 17301504 | tf_op jit(solution)/shard_map/concatenate | solution.py:49
  58.8 7.6 %copy.166 = bf16[2,3,8,176,512]{4,3,1,0,2:T(8,128)(2,1)} copy(bf16[2,3,8,176,512]{4,3,2,1,0:T(8,128)(2,1)} %pad_maximum_fusion.2) | data formatting | bytes 17301504 | tf_op jit(solution)/shard_map/concatenate | solution.py:49
  71.3 6.5 all-to-all-start.2
  77.8 195.6 %all-gather.1 = bf16[8,1,2048]{2,1,0:T(2,128)(2,1)S(1)} all-gather(bf16[1,1,2048]{2,1,0:T(2,128)(2,1)S(1)} %bitcast.240), channel_id=1, replica_groups=mesh['dp'=4,'expert'=8] {'expert'}, dimensions={0}, use_global_device_ids=true | all-gather | bytes 36864 | tf_op jit(solution)/shard_map/all_gather | solution.py:44
  273.4 8.5 %all_gather.19 = bf16[32,2048]{1,0:T(8,128)(2,1)S(1)} all-gather(bf16[8,2048]{1,0:T(8,128)(2,1)S(1)} %bitcast.236), channel_id=1, replica_groups=mesh['dp'=4,'expert'=8] {'dp'}, dimensions={0}, use_global_device_ids=true | all-gather | bytes 163840 | tf_op jit(solution)/shard_map/all_gather | solution.py:45
  320.0 11.4 %all-gather = f32[128,2,514]{2,0,1:T(8,128)S(1)} all-gather(f32[32,2,514]{2,0,1:T(8,128)S(1)} %pad_maximum_fusion.4), channel_id=2, replica_groups=mesh['dp'=4,'expert'=8] {'dp'}, dimensions={0}, use_global_device_ids=true | all-gather | bytes 657920 | tf_op jit(solution)/shard_map/all_gather | solution.py:190
  359.4 10.5 %select_subtract_fusion = s32[192]{0:T(256)S(1)} fusion(pred[192]{0:T(512)(128)(4,1)S(1)} %get-tuple-element.86, pred[192]{0:T(512)(128)(4,1)S(1)} %get-tuple-element.85, pred[192]{0:T(512)(128)(4,1)S(1)} %get-tuple-element.84, pred[192]{0:T(512)(128)(4,1)S(1)} %get-tuple-element.83, pred[192]{0:T(512)(128)(4,1)S(1)} %get-tuple-element.82, ...), kind=kLoop, calls=%fused_computation.212 | loop fusion | flops 3456 | bytes 4872 | tf_op jit(solution)/shard_map/sub | solution.py:253
  372.7 32.9 %all-reduce.8.cloned.1.call-done = f32[8,2048]{1,0:T(8,128)} async-done(((f32[8,2048]{1,0:T(8,128)}), f32[8,2048]{1,0:T(8,128)}) %all-reduce.8.cloned.1.call-update) | async-done | bytes 65552
  408.4 14.0 %all-gather.2 = bf16[8,1,2048]{2,1,0:T(2,128)(2,1)S(1)} all-gather(bf16[1,1,2048]{2,1,0:T(2,128)(2,1)S(1)} %convert_bitcast_fusion), channel_id=1, replica_groups=mesh['dp'=4,'expert'=8] {'expert'}, dimensions={0}, use_global_device_ids=true | all-gather | bytes 36864 | tf_op jit(solution)/shard_map/all_gather | solution.py:44
  422.4 8.4 %all_gather.23 = bf16[32,2048]{1,0:T(8,128)(2,1)S(1)} all-gather(bf16[8,2048]{1,0:T(8,128)(2,1)S(1)} %bitcast.237), channel_id=1, replica_groups=mesh['dp'=4,'expert'=8] {'dp'}, dimensions={0}, use_global_device_ids=true | all-gather | bytes 163840 | tf_op jit(solution)/shard_map/all_gather | solution.py:45
  430.9 4.9 convolution_bitcast_fusion
  435.8 6.9 convolution_bitcast_fusion.1
  443.4 46.9 %all-reduce.12.cloned.1.call-done = (f32[2,4,2816]{2,1,0:T(4,128)}, f32[4,2,16,1408]{3,2,1,0:T(8,128)}) async-done(((f32[2,4,2816]{2,1,0:T(4,128)}, f32[4,2,16,1408]{3,2,1,0:T(8,128)}), (f32[2,4,2816]{2,1,0:T(4,128)}, f32[4,2,16,1408]{3,2,1,0:T(8,128)})) %all-reduce.12.cloned.1.call-update) | async-done | bytes 811024 | tf_op jit(solution)/shard_map/psum | solution.py:272
  495.6 53.2 %all-reduce.10.cloned.1.call-done = f32[32,512]{1,0:T(8,128)} async-done(((f32[32,512]{1,0:T(8,128)}), f32[32,512]{1,0:T(8,128)}) %all-reduce.10.cloned.1.call-update) | async-done | bytes 65552
  554.3 6.3 gather_fusion.9
  560.6 6.1 broadcast_select_fusion.2
  573.1 95.0 %all-to-all-done.3 = bf16[8,3,176,512]{3,2,1,0:T(8,128)(2,1)} async-done(((bf16[8,3,176,512]{3,2,1,0:T(8,128)(2,1)}), bf16[8,3,176,512]{3,2,1,0:T(8,128)(2,1)}, u32[]{:S(2)}, u32[]{:S(2)}) %all-to-all-start.3) | async-done | bytes 4325408 | tf_op jit(solution)/shard_map/all_to_all | solution.py:100
  670.9 11.0 %broadcast_select_fusion = bf16[4,2,1408,512]{3,2,1,0:T(8,128)(2,1)} fusion(bf16[4,2,1408,512]{3,2,1,0:T(8,128)(2,1)} %param.34, pred[4]{0:T(512)(128)(4,1)S(1)} %iota_compare_fusion.9, bf16[2,1408,512]{2,1,0:T(8,128)(2,1)S(1)} %slice_bitcast_fusion), kind=kLoop, calls=%fused_computation.21 | loop fusion | flops 5767168 | bytes 25952260 | tf_op jit(solution)/shard_map/jit(_where)/select_n | solution.py:102
  (229 shorter events, 111.4 us)
Async XLA Ops:
  7.2 541.6 %copy-start = (bf16[2816,512]{1,0:T(8,128)(2,1)S(1)}, bf16[2816,512]{1,0:T(8,128)(2,1)}, u32[]{:S(2)}) copy-start(bf16[2816,512]{1,0:T(8,128)(2,1)} %param.37) | copy-start | bytes 8650756
  71.3 6.5 copy-start.10
  71.3 210.8 %copy-start.16 = (f32[2048]{0:T(1024)S(1)}, f32[2048]{0:T(1024)}, u32[]{:S(2)}) copy-start(f32[2048]{0:T(1024)} %param.21) | copy-start | bytes 24580
  71.3 213.0 %copy-start.17 = (s32[32,16]{0,1:T(8,128)S(1)}, s32[32,16]{0,1:T(8,128)}, u32[]{:S(2)}) copy-start(s32[32,16]{0,1:T(8,128)} %param.27) | copy-start | bytes 6148
  71.3 479.3 %all-to-all-start.2 = ((bf16[2,3,8,176,512]{4,3,1,0,2:T(8,128)(2,1)}), bf16[2,3,8,176,512]{4,3,1,0,2:T(8,128)(2,1)}, u32[]{:S(2)}, u32[]{:S(2)}) async-start(bf16[2,3,8,176,512]{4,3,1,0,2:T(8,128)(2,1)} %copy.166), calls=%async_computation.2 | async-start | bytes 17301504 | tf_op jit(solution)/shard_map/all_to_all | solution.py:52
  77.7 327.9 %all-reduce.8.cloned.1.call-start = ((), (), s32[]{:S(2)}) async-start(), calls=%async_computation.4 | async-start | bytes 131072
  286.8 55.8 %copy-start.1 = (bf16[512,512]{0,1:T(8,128)(2,1)}, bf16[512,512]{0,1:T(8,128)(2,1)S(1)}, u32[]{:S(2)}) copy-start(bf16[512,512]{0,1:T(8,128)(2,1)S(1)} %copy.145) | copy-start | bytes 1572868
  332.9 12.5 %copy-start.13 = (f32[8,2]{0,1:T(2,128)}, f32[8,2]{0,1:T(2,128)S(1)}, u32[]{:S(2)}) copy-start(f32[8,2]{0,1:T(2,128)S(1)} %get-tuple-element.98) | copy-start | bytes 196
  333.8 11.6 %copy-start.9 = (f32[4,8,2,1]{1,0,3,2:T(4,128)}, f32[4,8,2,1]{1,0,3,2:T(4,128)S(1)}, u32[]{:S(2)}) copy-start(f32[4,8,2,1]{1,0,3,2:T(4,128)S(1)} %copy.182) | copy-start | bytes 772
  338.2 10.3 %copy-start.14 = (f32[4,8,2,1]{1,0,3,2:T(4,128)S(1)}, f32[4,8,2,1]{1,0,3,2:T(4,128)}, u32[]{:S(2)}) copy-start(f32[4,8,2,1]{1,0,3,2:T(4,128)} %copy.183) | copy-start | bytes 772
  338.2 14.2 %copy-start.21 = (s32[32,6]{0,1:T(8,128)S(1)}, s32[32,6]{0,1:T(8,128)}, u32[]{:S(2)}) copy-start(s32[32,6]{0,1:T(8,128)} %param.30) | copy-start | bytes 2308
  338.2 14.5 %copy-start.20 = (s32[32]{0:T(128)S(1)}, s32[32]{0:T(128)}, u32[]{:S(2)}) copy-start(s32[32]{0:T(128)} %copy-done.19) | copy-start | bytes 388
  338.2 33.5 %copy-start.22 = (f32[32,6]{0,1:T(8,128)S(1)}, f32[32,6]{0,1:T(8,128)}, u32[]{:S(2)}) copy-start(f32[32,6]{0,1:T(8,128)} %param.31) | copy-start | bytes 2308
  338.2 33.8 %copy-start.28 = (u32[32]{0:T(128)S(1)}, u32[32]{0:T(128)}, u32[]{:S(2)}) copy-start(u32[32]{0:T(128)} %constant.206) | copy-start | bytes 388
  338.3 67.3 %copy-start.11 = (bf16[1,2048]{1,0:T(2,128)(2,1)S(1)}, bf16[1,2048]{1,0:T(2,128)(2,1)}, u32[]{:S(2)}) copy-start(bf16[1,2048]{1,0:T(2,128)(2,1)} %param.20) | copy-start | bytes 12292
  338.3 70.1 %copy-start.18 = (f32[2048]{0:T(1024)S(1)}, f32[2048]{0:T(1024)}, u32[]{:S(2)}) copy-start(f32[2048]{0:T(1024)} %param.29) | copy-start | bytes 24580
  352.4 137.9 %all-reduce.12.cloned.1.call-start = ((), (), s32[]{:S(2)}) async-start(), calls=%async_computation.6 | async-start | bytes 1622016 | tf_op jit(solution)/shard_map/psum | solution.py:272
  442.7 106.1 %all-reduce.10.cloned.1.call-start = ((), (), s32[]{:S(2)}) async-start(), calls=%async_computation.5 | async-start | bytes 131072
  490.3 4.7 copy-start.24
  490.3 58.5 %copy-start.12 = (f32[2,4,2816]{2,1,0:T(4,128)S(1)}, f32[2,4,2816]{2,1,0:T(4,128)}, u32[]{:S(2)}) copy-start(f32[2,4,2816]{2,1,0:T(4,128)} %get-tuple-element.87) | copy-start | bytes 270340
  550.6 16.1 %all-to-all-start.1 = ((f32[4,1,512]{2,1,0:T(1,128)}), f32[4,1,512]{2,1,0:T(1,128)S(1)}, u32[]{:S(2)}, u32[]{:S(2)}) async-start(f32[4,1,512]{2,1,0:T(1,128)} %copy.164), calls=%async_computation.1 | async-start | bytes 16384 | tf_op jit(solution)/shard_map/all_to_all | solution.py:281
  566.7 101.4 %all-to-all-start.3 = ((bf16[8,3,176,512]{3,2,1,0:T(8,128)(2,1)}), bf16[8,3,176,512]{3,2,1,0:T(8,128)(2,1)}, u32[]{:S(2)}, u32[]{:S(2)}) async-start(bf16[8,3,176,512]{3,2,1,0:T(8,128)(2,1)} %broadcast_select_fusion.2), calls=%async_computation.3 | async-start | bytes 8650752 | tf_op jit(solution)/shard_map/all_to_all | solution.py:100
  670.6 11.3 %slice-start = ((s8[5767168]{0:T(1024)(128)(4,1)}), s8[4194304]{0:T(1024)(128)(4,1)S(1)}, s32[]{:S(2)}) async-start(s8[5767168]{0:T(1024)(128)(4,1)} %bitcast.223), calls=%async_computation.7 | async-start | bytes 8388608
  670.9 11.0 %slice-start.1 = ((s8[5767168]{0:T(1024)(128)(4,1)}), s8[1572864]{0:T(1024)(128)(4,1)S(1)}, s32[]{:S(2)}) async-start(s8[5767168]{0:T(1024)(128)(4,1)} %bitcast.223), calls=%async_computation.8 | async-start | bytes 3145728
  (13 other events, 18.8 us)
Sparse Core Ops, SparseCore 0:
  352.5 53.0 all-reduce.7
  442.8 47.3 all-reduce.11
  495.1 53.6 all-reduce.9
where the time goes:
time: 694 us; the launch traced here: 692 us
  blocking collectives  238 us (34%)
  waiting for transfers between devices  228 us (33%)
  local copies, waits for them, and re-layouts  79.7 us (11%)
  other arithmetic  79.7 us (11%)
  matrix products  33.6 us (5%)
  between operations  18.1 us (3%)
  starting transfers between devices  14.8 us (2%)
    all_gather x2, blocking collectives, gather_rows(): by_expert = lax.all_gather(rows, 'expert', axis=0, tiled=True)  210 us
    all_to_all x1, waiting for transfers between devices, migrate(): lax.all_to_all(out_a, 'expert', split_axis=0, concat_axis=2, tiled=True)  95 us
    unnamed x5, waiting for transfers between devices  86.2 us
    psum x1, waiting for transfers between devices, local(): routed_sum, shared_sum = lax.psum((routed_part, shared_part), 'dp')  46.9 us
    gather x5, local copies, waits for them, and re-layouts, spread_slots(): chosen = jnp.concatenate([gate_up[picks], down[picks][:, None]], axis=1)  25.9 us
    all_gather x2, blocking collectives, gather_rows(): return lax.all_gather(by_expert, 'dp', axis=0, tiled=True)  16.9 us
  transfers between devices with their start and end apart: 6, of which 4 were waited for; matrix products, arithmetic and copies ran while one was open for 16% of the time, Pallas kernels for 0%

commit v1 on v0

--- a/solution.py
+++ b/solution.py
@@ -41,7 +41,14 @@
 
 
 def gather_rows(rows):
-    by_expert = lax.all_gather(rows, "expert", axis=0, tiled=True)
+    ring = [rows]
+    for hop in range(7):
+        ring.append(lax.ppermute(ring[-1], "expert", [(dev, (dev + 1) % 8) for dev in range(8)]))
+    by_expert = jnp.roll(
+        jnp.concatenate(ring[::-1], axis=0),
+        (lax.axis_index("expert") + 1) * ring[0].shape[0],
+        axis=0,
+    )
     return lax.all_gather(by_expert, "dp", axis=0, tiled=True)
 
 

time: 694 us -> 721 us (1.039)
  blocking collectives: 238 us -> 28.3 us
  waiting for transfers between devices: 228 us -> 425 us
  starting transfers between devices: 14.8 us -> 54.5 us
    all_gather x2 -> x0, blocking collectives: 210 us -> none  [gather_rows(): by_expert = lax.all_gather(rows, 'expert', axis=0, tiled=True)]
    ppermute x0 -> x14, waiting for transfers between devices: none -> 182 us  [gather_rows(): lax.ppermute(ring[-1], 'expert', [(dev, (dev + 1) % 8) for dev in range(8)])]
    ppermute x0 -> x14, starting transfers between devices: none -> 39.7 us  [gather_rows(): lax.ppermute(ring[-1], 'expert', [(dev, (dev + 1) % 8) for dev in range(8)])]
    unnamed x5, waiting for transfers between devices: 86.2 us -> 101 us
  transfers between devices with their start and end apart: 6 -> 20, of which waited for: 4 -> 17; matrix products, arithmetic and copies ran while one was open for 16% -> 16% of each run, Pallas kernels for 0% -> 0%
where the time goes in v1:
time: 721 us; the launch traced here: 718 us
  waiting for transfers between devices  425 us (59%)
  local copies, waits for them, and re-layouts  79.9 us (11%)
  other arithmetic  79.1 us (11%)
  starting transfers between devices  54.5 us (8%)
  matrix products  33.4 us (5%)
  blocking collectives  28.3 us (4%)
  between operations  18.3 us (3%)
    ppermute x14, waiting for transfers between devices, gather_rows(): lax.ppermute(ring[-1], 'expert', [(dev, (dev + 1) % 8) for dev in range(8)])  182 us
    unnamed x5, waiting for transfers between devices  101 us
    all_to_all x1, waiting for transfers between devices, migrate(): lax.all_to_all(out_a, 'expert', split_axis=0, concat_axis=2, tiled=True)  95 us
    psum x1, waiting for transfers between devices, local(): routed_sum, shared_sum = lax.psum((routed_part, shared_part), 'dp')  46.1 us
    ppermute x14, starting transfers between devices, gather_rows(): lax.ppermute(ring[-1], 'expert', [(dev, (dev + 1) % 8) for dev in range(8)])  39.7 us
    gather x5, local copies, waits for them, and re-layouts, spread_slots(): chosen = jnp.concatenate([gate_up[picks], down[picks][:, None]], axis=1)  25.9 us
    all_gather x2, blocking collectives, gather_rows(): return lax.all_gather(by_expert, 'dp', axis=0, tiled=True)  17.1 us
  transfers between devices with their start and end apart: 20, of which 17 were waited for; matrix products, arithmetic and copies ran while one was open for 16% of the time, Pallas kernels for 0%

profile of v1, /device:TPU:0, one launch (start us, length us, event | category | flops | bytes accessed | tf_op | source)
XLA Modules:
  0.0 718.4 jit_solution(5115303230846686890)
XLA Ops:
  18.3 5.9 mini-gather-slice.2
  24.2 5.2 mini-gather-slice.3
  30.9 5.2 gather_fusion.11
  40.8 5.0 gather_fusion.8
  45.8 5.6 pad_maximum_fusion.3
  51.4 7.7 %pad_maximum_fusion.2 = bf16[2,3,8,176,512]{4,3,2,1,0:T(8,128)(2,1)} fusion(bf16[2,1,8,176,512]{4,3,2,1,0:T(8,128)(2,1)} %bitcast.220, bf16[2,2,8,176,512]{4,3,2,1,0:T(8,128)(2,1)} %bitcast.216), kind=kLoop, calls=%fused_computation.22 | loop fusion | flops 4325376 | bytes 17301504 | tf_op jit(solution)/shard_map/concatenate | solution.py:56
  59.1 7.6 %copy.166 = bf16[2,3,8,176,512]{4,3,1,0,2:T(8,128)(2,1)} copy(bf16[2,3,8,176,512]{4,3,2,1,0:T(8,128)(2,1)} %pad_maximum_fusion.2) | data formatting | bytes 17301504 | tf_op jit(solution)/shard_map/concatenate | solution.py:56
  71.6 6.5 all-to-all-start.2
  82.7 139.2 %collective-permute-done = bf16[1,2048]{1,0:T(2,128)(2,1)S(1)} collective-permute-done((bf16[1,2048]{1,0:T(2,128)(2,1)S(1)}, bf16[1,2048]{1,0:T(2,128)(2,1)S(1)}, u32[]{:S(2)}, u32[]{:S(2)}) %collective-permute-start) | collective-permute-done | bytes 4128 | tf_op jit(solution)/shard_map/ppermute | solution.py:46
  231.9 36.1 %collective-permute-start.3 = (bf16[1,2048]{1,0:T(2,128)(2,1)S(1)}, bf16[1,2048]{1,0:T(2,128)(2,1)S(1)}, u32[]{:S(2)}, u32[]{:S(2)}) collective-permute-start(bf16[1,2048]{1,0:T(2,128)(2,1)S(1)} %collective-permute-done.2), channel_id=1, source_target_pairs={{0,1},{1,2},{2,3},{3,4},{4,5},{5,6},{6,7},{7,0},{8,9},{9,10},{10,1... | collective-permute-start | bytes 12296 | tf_op jit(solution)/shard_map/ppermute | solution.py:46
  283.6 8.7 %all_gather.12 = bf16[32,2048]{1,0:T(8,128)(2,1)S(1)} all-gather(bf16[8,2048]{1,0:T(8,128)(2,1)S(1)} %fusion.26), channel_id=1, replica_groups=mesh['dp'=4,'expert'=8] {'dp'}, dimensions={0}, use_global_device_ids=true | all-gather | bytes 163840 | tf_op jit(solution)/shard_map/all_gather | solution.py:52
  323.7 11.2 %all-gather = f32[128,2,514]{2,0,1:T(8,128)S(1)} all-gather(f32[32,2,514]{2,0,1:T(8,128)S(1)} %pad_maximum_fusion.4), channel_id=2, replica_groups=mesh['dp'=4,'expert'=8] {'dp'}, dimensions={0}, use_global_device_ids=true | all-gather | bytes 657920 | tf_op jit(solution)/shard_map/all_gather | solution.py:197
  358.9 48.2 %all-reduce.8.cloned.1.call-done = f32[8,2048]{1,0:T(8,128)} async-done(((f32[8,2048]{1,0:T(8,128)}), f32[8,2048]{1,0:T(8,128)}) %all-reduce.8.cloned.1.call-update) | async-done | bytes 65552
  414.8 10.6 %select_subtract_fusion = s32[192]{0:T(256)S(1)} fusion(pred[192]{0:T(512)(128)(4,1)S(1)} %get-tuple-element.87, pred[192]{0:T(512)(128)(4,1)S(1)} %get-tuple-element.86, pred[192]{0:T(512)(128)(4,1)S(1)} %get-tuple-element.85, pred[192]{0:T(512)(128)(4,1)S(1)} %get-tuple-element.84, pred[192]{0:T(512)(128)(4,1)S(1)} %get-tuple-element.83, ...), kind=kLoop, calls=%fused_computation.216 | loop fusion | flops 3456 | bytes 4872 | tf_op jit(solution)/shard_map/sub | solution.py:260
  425.5 4.8 collective-permute-done.9
  450.0 8.4 %all_gather.15 = bf16[32,2048]{1,0:T(8,128)(2,1)S(1)} all-gather(bf16[8,2048]{1,0:T(8,128)(2,1)S(1)} %fusion.25), channel_id=1, replica_groups=mesh['dp'=4,'expert'=8] {'dp'}, dimensions={0}, use_global_device_ids=true | all-gather | bytes 163840 | tf_op jit(solution)/shard_map/all_gather | solution.py:52
  458.5 4.9 convolution_bitcast_fusion
  463.4 6.9 convolution_bitcast_fusion.1
  470.9 46.1 %all-reduce.12.cloned.1.call-done = (f32[2,4,2816]{2,1,0:T(4,128)}, f32[4,2,16,1408]{3,2,1,0:T(8,128)}) async-done(((f32[2,4,2816]{2,1,0:T(4,128)}, f32[4,2,16,1408]{3,2,1,0:T(8,128)}), (f32[2,4,2816]{2,1,0:T(4,128)}, f32[4,2,16,1408]{3,2,1,0:T(8,128)})) %all-reduce.12.cloned.1.call-update) | async-done | bytes 811024 | tf_op jit(solution)/shard_map/psum | solution.py:279
  522.4 53.1 %all-reduce.10.cloned.1.call-done = f32[32,512]{1,0:T(8,128)} async-done(((f32[32,512]{1,0:T(8,128)}), f32[32,512]{1,0:T(8,128)}) %all-reduce.10.cloned.1.call-update) | async-done | bytes 65552
  581.0 6.3 gather_fusion.9
  587.4 6.1 broadcast_select_fusion.2
  599.9 95.0 %all-to-all-done.3 = bf16[8,3,176,512]{3,2,1,0:T(8,128)(2,1)} async-done(((bf16[8,3,176,512]{3,2,1,0:T(8,128)(2,1)}), bf16[8,3,176,512]{3,2,1,0:T(8,128)(2,1)}, u32[]{:S(2)}, u32[]{:S(2)}) %all-to-all-start.3) | async-done | bytes 4325408 | tf_op jit(solution)/shard_map/all_to_all | solution.py:107
  697.7 11.0 %broadcast_select_fusion = bf16[4,2,1408,512]{3,2,1,0:T(8,128)(2,1)} fusion(bf16[4,2,1408,512]{3,2,1,0:T(8,128)(2,1)} %param.36, pred[4]{0:T(512)(128)(4,1)S(1)} %iota_compare_fusion.9, bf16[2,1408,512]{2,1,0:T(8,128)(2,1)S(1)} %slice_bitcast_fusion), kind=kLoop, calls=%fused_computation.21 | loop fusion | flops 5767168 | bytes 25952260 | tf_op jit(solution)/shard_map/jit(_where)/select_n | solution.py:109
  (249 shorter events, 157.4 us)
Async XLA Ops:
  7.2 568.4 %copy-start = (bf16[2816,512]{1,0:T(8,128)(2,1)S(1)}, bf16[2816,512]{1,0:T(8,128)(2,1)}, u32[]{:S(2)}) copy-start(bf16[2816,512]{1,0:T(8,128)(2,1)} %param.39) | copy-start | bytes 8650756
  71.6 207.6 %copy-start.17 = (s32[32,6]{0,1:T(8,128)S(1)}, s32[32,6]{0,1:T(8,128)}, u32[]{:S(2)}) copy-start(s32[32,6]{0,1:T(8,128)} %param.32) | copy-start | bytes 2308
  71.6 505.8 %all-to-all-start.2 = ((bf16[2,3,8,176,512]{4,3,1,0,2:T(8,128)(2,1)}), bf16[2,3,8,176,512]{4,3,1,0,2:T(8,128)(2,1)}, u32[]{:S(2)}, u32[]{:S(2)}) async-start(bf16[2,3,8,176,512]{4,3,1,0,2:T(8,128)(2,1)} %copy.166), calls=%async_computation.2 | async-start | bytes 17301504 | tf_op jit(solution)/shard_map/all_to_all | solution.py:59
  78.0 329.0 %all-reduce.8.cloned.1.call-start = ((), (), s32[]{:S(2)}) async-start(), calls=%async_computation.4 | async-start | bytes 131072
  78.1 143.8 %collective-permute-start = (bf16[1,2048]{1,0:T(2,128)(2,1)S(1)}, bf16[1,2048]{1,0:T(2,128)(2,1)S(1)}, u32[]{:S(2)}, u32[]{:S(2)}) collective-permute-start(bf16[1,2048]{1,0:T(2,128)(2,1)S(1)} %copy-done.8), channel_id=1, source_target_pairs={{0,1},{1,2},{2,3},{3,4},{4,5},{5,6},{6,7},{7,0},{8,9},{9,10},{10,1... | collective-permute-start | bytes 12296 | tf_op jit(solution)/shard_map/ppermute | solution.py:46
  78.8 200.4 %copy-start.19 = (f32[32]{0:T(128)}, f32[32]{0:T(128)S(1)}, u32[]{:S(2)}) copy-start(f32[32]{0:T(128)S(1)} %multiply_exponential_fusion) | copy-start | bytes 388
  221.9 5.0 collective-permute-start.1
  226.9 5.0 collective-permute-start.2
  231.9 36.9 %collective-permute-start.3 = (bf16[1,2048]{1,0:T(2,128)(2,1)S(1)}, bf16[1,2048]{1,0:T(2,128)(2,1)S(1)}, u32[]{:S(2)}, u32[]{:S(2)}) collective-permute-start(bf16[1,2048]{1,0:T(2,128)(2,1)S(1)} %collective-permute-done.2), channel_id=1, source_target_pairs={{0,1},{1,2},{2,3},{3,4},{4,5},{5,6},{6,7},{7,0},{8,9},{9,10},{10,1... | collective-permute-start | bytes 12296 | tf_op jit(solution)/shard_map/ppermute | solution.py:46
  268.8 4.9 collective-permute-start.4
  273.7 4.9 collective-permute-start.5
  278.6 4.9 collective-permute-start.6
  341.3 99.1 %copy-start.18 = (f32[32,6]{0,1:T(8,128)S(1)}, f32[32,6]{0,1:T(8,128)}, u32[]{:S(2)}) copy-start(f32[32,6]{0,1:T(8,128)} %param.33) | copy-start | bytes 2308
  353.9 163.1 %all-reduce.12.cloned.1.call-start = ((), (), s32[]{:S(2)}) async-start(), calls=%async_computation.6 | async-start | bytes 1622016 | tf_op jit(solution)/shard_map/psum | solution.py:279
  409.9 4.9 collective-permute-start.7
  414.8 10.6 %collective-permute-start.8 = (bf16[1,2048]{1,0:T(2,128)(2,1)S(1)}, bf16[1,2048]{1,0:T(2,128)(2,1)S(1)}, u32[]{:S(2)}, u32[]{:S(2)}) collective-permute-start(bf16[1,2048]{1,0:T(2,128)(2,1)S(1)} %collective-permute-done.7), channel_id=1, source_target_pairs={{0,1},{1,2},{2,3},{3,4},{4,5},{5,6},{6,7},{7,0},{8,9},{9,10},{10,1... | collective-permute-start | bytes 12296 | tf_op jit(solution)/shard_map/ppermute | solution.py:46
  425.4 4.9 collective-permute-start.9
  430.4 4.9 collective-permute-start.10
  435.2 4.9 collective-permute-start.11
  440.1 4.9 collective-permute-start.12
  445.0 4.9 collective-permute-start.13
  470.3 105.3 %all-reduce.10.cloned.1.call-start = ((), (), s32[]{:S(2)}) async-start(), calls=%async_computation.5 | async-start | bytes 131072
  577.4 16.1 %all-to-all-start.1 = ((f32[4,1,512]{2,1,0:T(1,128)}), f32[4,1,512]{2,1,0:T(1,128)S(1)}, u32[]{:S(2)}, u32[]{:S(2)}) async-start(f32[4,1,512]{2,1,0:T(1,128)} %copy.164), calls=%async_computation.1 | async-start | bytes 16384 | tf_op jit(solution)/shard_map/all_to_all | solution.py:288
  593.5 101.4 %all-to-all-start.3 = ((bf16[8,3,176,512]{3,2,1,0:T(8,128)(2,1)}), bf16[8,3,176,512]{3,2,1,0:T(8,128)(2,1)}, u32[]{:S(2)}, u32[]{:S(2)}) async-start(bf16[8,3,176,512]{3,2,1,0:T(8,128)(2,1)} %broadcast_select_fusion.2), calls=%async_computation.3 | async-start | bytes 8650752 | tf_op jit(solution)/shard_map/all_to_all | solution.py:107
  (23 other events, 423.5 us)
Sparse Core Ops, SparseCore 0:
  354.0 52.9 all-reduce.7
  470.4 46.6 all-reduce.11
  521.8 53.6 all-reduce.9
